TPU v7x, 32 devices: a whole 2x2x4 slice. The times are simulated.
32 devices in a mesh: blk: 8 (over z, y), corpus: 4 (over x, core).
Axes of the slice: x: 2, y: 2, z: 4, core: 2. Of those that a mesh axis runs over, the one named last changes fastest.
Arguments:
- queries: bfloat16 [1024, 4096], P('blk', 'corpus'), may hold values from -12 to 12
- passages: bfloat16 [1024, 4096], P('blk', 'corpus'), may hold values from -4 to 4
- table: bfloat16 [1024, 4096], P('corpus'), may hold values from -4 to 4
- neg_owner: int32 [1024, 7], P('blk'), may hold values from 0 to 3, as said below
- neg_row: int32 [1024, 7], P('blk'), may hold values from 0 to 255
- positive: int32 [1024], P('blk'), may hold values from 0 to 1023, each once
- loss_weight: float32 [1024], P('blk'), may hold values from 32 to 256
Outputs:
- losses: float32 [1024], P(('blk', 'corpus'))
- query_grad: float32 [1024, 4096], P('blk', 'corpus')
- passage_grad: float32 [1024, 4096], P('blk', 'corpus')
- table_grad: float32 [1024, 4096], P('corpus', 'blk')
Inputs may be any that keep to these rules, and one draw needn't show every extreme that they name: `neg_owner`: among the 896 references of the queries of one index of blk (aligned blocks of 128 queries), one shard is named exactly 448 times and no shard more often.
All inputs are finite; a program needn't handle non-finite values.
Results may differ from a plain program's by a relative error of at most 0.0065.
Values may be sent and summed in bfloat16 or wider, within the bound.
No kernel may reach another device: no remote copies, remote signals or barrier semaphores. Data moves between devices by JAX's collectives and lax.ppermute only.
A program may use at most 128 MiB of HBM per device.

v0:
```python
import jax
import jax.numpy as jnp
from jax import lax
from jax.sharding import PartitionSpec as P


def hi_lo(mixing):
    upper = mixing.astype(jnp.bfloat16)
    lower = (mixing - upper.astype(jnp.float32)).astype(jnp.bfloat16)
    return (upper, lower)


def per_device(queries, passages, table, neg_owner, neg_row, positive, loss_weight):
    q_rows, col_width = queries.shape
    owner_count = lax.axis_size("corpus")
    blk_count = lax.axis_size("blk")
    factor = (col_width * owner_count) ** (-0.5)
    rows_shard = table.shape[0]
    table_rows = owner_count * rows_shard
    owner_index = lax.axis_index("corpus")
    blk_index = lax.axis_index("blk")
    table_cols = lax.all_to_all(table, "corpus", split_axis=1, concat_axis=0, tiled=True)
    all_passages = lax.all_gather(passages, "blk", axis=0, tiled=True)
    all_queries = lax.all_gather(queries, "blk", axis=0, tiled=True)
    ids = neg_owner * rows_shard + neg_row
    all_ids = lax.all_gather(ids, "blk", axis=0, tiled=True)
    all_rows = all_passages.shape[0]
    logits = lax.dot_general(
        queries, all_passages, (((1,), (1,)), ((), ())), preferred_element_type=jnp.float32
    )
    table_scores = lax.dot_general(
        queries, table_cols, (((1,), (1,)), ((), ())), preferred_element_type=jnp.float32
    )
    row_iota = jnp.arange(table_rows, dtype=jnp.int32)
    picks = ids[:, :, None] == row_iota[None, None, :]
    hard_logits = jnp.sum(jnp.where(picks, table_scores[:, None, :], 0.0), axis=2)
    logits, hard_logits = lax.psum((logits, hard_logits), "corpus")
    logits = logits * factor
    hard_logits = hard_logits * factor
    row_top = jnp.maximum(jnp.max(logits, axis=1), jnp.max(hard_logits, axis=1))
    log_total = row_top + jnp.log(
        jnp.sum(jnp.exp(logits - row_top[:, None]), axis=1)
        + jnp.sum(jnp.exp(hard_logits - row_top[:, None]), axis=1)
    )
    one_hot = positive[:, None] == jnp.arange(all_rows, dtype=jnp.int32)[None, :]
    losses = log_total - jnp.sum(jnp.where(one_hot, logits, 0.0), axis=1)
    share = q_rows // owner_count
    loss_share = lax.dynamic_slice_in_dim(losses, owner_index * share, share)
    weighting = (loss_weight * factor)[:, None]
    soft_grad = (
        weighting * (jnp.exp(logits - log_total[:, None]) - one_hot.astype(jnp.float32))
    ).astype(jnp.bfloat16)
    hard_grad = (weighting * jnp.exp(hard_logits - log_total[:, None])).astype(jnp.bfloat16)
    mixing = jnp.sum(jnp.where(picks, hard_grad.astype(jnp.float32)[:, :, None], 0.0), axis=1)
    mix_hi, mix_lo = hi_lo(mixing)
    left = jnp.concatenate([soft_grad, mix_hi, mix_lo], axis=1)
    right = jnp.concatenate([all_passages, table_cols, table_cols], axis=0)
    query_grad = jnp.dot(left, right, preferred_element_type=jnp.float32)
    soft_cols = lax.all_to_all(soft_grad, "blk", split_axis=1, concat_axis=0, tiled=True)
    passage_grad = lax.dot_general(
        soft_cols, all_queries, (((0,), (0,)), ((), ())), preferred_element_type=jnp.float32
    )
    all_hard = lax.all_gather(hard_grad, "blk", axis=0, tiled=True)
    per_col = blk_count // owner_count
    piece_width = col_width // per_col
    shard = blk_index // per_col
    part = blk_index % per_col
    shard_iota = shard * rows_shard + jnp.arange(rows_shard, dtype=jnp.int32)
    shard_picks = all_ids[:, :, None] == shard_iota[None, None, :]
    shard_mix = jnp.sum(
        jnp.where(shard_picks, all_hard.astype(jnp.float32)[:, :, None], 0.0), axis=1
    )
    shard_hi, shard_lo = hi_lo(shard_mix)
    query_part = lax.dynamic_slice_in_dim(all_queries, part * piece_width, piece_width, axis=1)
    dims = (((0,), (0,)), ((), ()))
    piece = lax.dot_general(
        shard_hi, query_part, dims, preferred_element_type=jnp.float32
    ) + lax.dot_general(shard_lo, query_part, dims, preferred_element_type=jnp.float32)
    perm = []
    for b in range(blk_count):
        for c in range(owner_count):
            dest_b = c * per_col + b % per_col
            dest_c = b // per_col
            perm.append((b * owner_count + c, dest_b * owner_count + dest_c))
    table_grad = lax.ppermute(piece, ("blk", "corpus"), perm)
    return (loss_share, query_grad, passage_grad, table_grad)


def solution(mesh):
    placed = (
        P("blk", "corpus"),
        P("blk", "corpus"),
        P("corpus", None),
        P("blk", None),
        P("blk", None),
        P("blk"),
        P("blk"),
    )
    return jax.shard_map(
        per_device,
        mesh=mesh,
        in_specs=placed,
        out_specs=(
            P(("blk", "corpus")),
            P("blk", "corpus"),
            P("blk", "corpus"),
            P("corpus", "blk"),
        ),
        check_vma=False,
    )
```

profile of v0, /device:TPU:2, one launch (start us, length us, event | category | flops | bytes accessed | tf_op | source)
XLA Modules:
  0.0 190.5 jit_solution(2006193391956256831)
XLA Ops:
  7.2 0.0 all-gather.3.cloned.1.call-start
  7.2 0.7 all-gather.3.cloned.1.call-update
  7.9 3.3 %copy.26 = bf16[256,4096]{0,1:T(8,128)(2,1)S(1)} copy(bf16[256,4096]{1,0:T(8,128)(2,1)} %param.9) | data formatting | bytes 4194304 | tf_op args[2]
  11.2 2.5 %copy.27 = bf16[256,4,1024]{2,0,1:T(8,128)(2,1)} copy(bf16[256,4,1024]{0,2,1:T(8,128)(2,1)S(1)} %bitcast.20) | data formatting | bytes 4194304 | tf_op jit(solution)/shard_map/all_to_all | solution.py:22
  13.7 0.0 copy-start.2
  13.7 3.7 %all-to-all-start = ((bf16[256,4,1024]{2,0,1:T(8,128)(2,1)}), bf16[256,4,1024]{2,0,1:T(8,128)(2,1)S(1)}, u32[]{:S(2)}, u32[]{:S(2)}) async-start(bf16[256,4,1024]{2,0,1:T(8,128)(2,1)} %copy.27), calls=%async_computation | async-start | bytes 4194304 | tf_op jit(solution)/shard_map/all_to_all | solution.py:22
  17.4 0.0 copy-start.8
  17.4 0.0 copy-start.9
  17.5 0.0 copy-start.10
  17.5 0.0 copy-start.3
  17.5 0.0 all-reduce.2.cloned.1.call-start
  17.5 42.9 %all-gather.3.cloned.1.call-done = bf16[1024,1024]{1,0:T(8,128)(2,1)} async-done(((bf16[128,1024]{1,0:T(8,128)(2,1)}), bf16[1024,1024]{1,0:T(8,128)(2,1)}) %all-gather.3.cloned.1.call-update) | async-done | bytes 2097168 | tf_op jit(solution)/shard_map/all_gather | solution.py:23
  60.5 0.0 copy-done.2
  60.5 3.2 %fusion.21 = f32[128,1024]{1,0:T(8,128)} fusion(bf16[128,1024]{1,0:T(8,128)(2,1)S(1)} %copy-done.2, bf16[1024,1024]{1,0:T(8,128)(2,1)} %all-gather.3.cloned.1.call-done), kind=kOutput, calls=%fused_computation.41 | convolution fusion | flops 268435456 | bytes 2883584 | tf_op jit(solution)/shard_map/dot_general | solution.py:28
  63.7 0.0 all-reduce.2.cloned.1.call-update
  63.7 0.0 all-gather.5.cloned.1.call-start
  63.7 0.7 all-gather.5.cloned.1.call-update
  64.4 0.0 copy-start.7
  64.5 0.0 copy-done.8
  64.5 0.0 copy-done.9
  64.5 30.6 %all_gather.14 = s32[1024,7]{0,1:T(8,128)S(1)} all-gather(s32[128,7]{0,1:T(8,128)S(1)} %multiply_add_fusion), channel_id=1, replica_groups=mesh['blk'=8,'corpus'=4] {'blk'}, dimensions={0}, use_global_device_ids=true | all-gather | bytes 32256 | tf_op jit(solution)/shard_map/all_gather | solution.py:26
  95.1 0.0 copy-done.10
  95.1 0.0 all-to-all-done
  95.1 0.0 copy-done.3
  95.1 0.8 fusion.22
  96.0 0.6 select_reduce_fusion.2
  96.6 5.9 %psum.15 = f32[128,7]{0,1:T(8,128)S(1)} all-reduce(f32[128,7]{0,1:T(8,128)S(1)} %select_reduce_fusion.2), channel_id=1, replica_groups=mesh['blk'=8,'corpus'=4] {'corpus'}, use_global_device_ids=true, to_apply=%region_3.4 | all-reduce | flops 896 | bytes 7168 | tf_op jit(solution)/shard_map/psum | solution.py:37
  102.5 0.0 all-reduce.2.cloned.1.call-done
  102.5 1.2 multiply_reduce_fusion
  103.7 0.0 copy-done.7
  103.7 1.4 select_reduce_fusion.3
  105.1 2.1 %copy_bitcast_fusion = bf16[128,8,128]{2,0,1:T(8,128)(2,1)} fusion(s32[128]{0:T(128)S(1)} %copy-done.7, f32[128]{0:T(128)S(1)} %get-tuple-element.11, f32[128,1024]{1,0:T(8,128)} %all-reduce.2.cloned.1.call-done, f32[128]{0:T(128)S(1)} %broadcast_multiply_fusion), kind=kLoop, calls=%fused_computation.26 | loop fusion | flops 917504 | bytes 787968 | tf_op jit(solution)/shard_map/all_to_all | solution.py:59
  107.2 3.4 %all-to-all-start.1 = ((bf16[128,8,128]{2,0,1:T(8,128)(2,1)}), bf16[128,8,128]{2,0,1:T(8,128)(2,1)S(1)}, u32[]{:S(2)}, u32[]{:S(2)}) async-start(bf16[128,8,128]{2,0,1:T(8,128)(2,1)} %copy_bitcast_fusion), calls=%async_computation.1 | async-start | bytes 524288 | tf_op jit(solution)/shard_map/all_to_all | solution.py:59
  110.6 33.2 %all_gather.15 = bf16[1024,7]{0,1:T(8,128)(2,1)S(1)} all-gather(bf16[128,7]{0,1:T(8,128)(2,1)S(1)} %get-tuple-element.9), channel_id=1, replica_groups=mesh['blk'=8,'corpus'=4] {'blk'}, dimensions={0}, use_global_device_ids=true | all-gather | bytes 16128 | tf_op jit(solution)/shard_map/all_gather | solution.py:63
  143.8 0.5 select_reduce_fusion.1
  144.3 0.9 subtract_convert_fusion.2
  145.2 2.5 %select_reduce_fusion = f32[1024,256]{1,0:T(8,128)S(1)} fusion(f32[1024,7]{0,1:T(8,128)S(1)} %convert_element_type.40, s32[256]{0:T(256)S(1)} %iota_add_fusion, s32[1024,7]{0,1:T(8,128)S(1)} %all_gather.14), kind=kLoop, calls=%fused_computation | loop fusion | flops 5242880 | bytes 1106944 | tf_op jit(solution)/shard_map/reduce_sum | solution.py:70
  147.7 3.9 %all-gather.5.cloned.1.call-done = bf16[1024,1024]{1,0:T(8,128)(2,1)} async-done(((bf16[128,1024]{1,0:T(8,128)(2,1)}), bf16[1024,1024]{1,0:T(8,128)(2,1)}) %all-gather.5.cloned.1.call-update) | async-done | bytes 2097168 | tf_op jit(solution)/shard_map/all_gather | solution.py:24
  151.7 0.0 copy-start
  151.7 1.8 fusion.7
  153.5 0.1 copy-done
  153.6 0.0 copy-start.1
  153.6 0.0 copy-start.4
  153.6 0.0 copy-start.5
  153.6 0.0 copy-start.6
  153.6 1.3 convolution_add_fusion
  154.9 3.7 %collective-permute-start = (f32[256,512]{1,0:T(8,128)}, f32[256,512]{1,0:T(8,128)S(1)}, u32[]{:S(2)}, u32[]{:S(2)}) collective-permute-start(f32[256,512]{1,0:T(8,128)} %convolution_add_fusion), channel_id=1, source_target_pairs={{0,0},{1,8},{2,16},{3,24},{4,4},{5,12},{6,20},{7,28},{8,1},{9,9},{... | collective-permute-start | bytes 1572872 | tf_op jit(solution)/shard_map/ppermute | solution.py:85
  158.6 0.0 copy-done.1
  158.7 0.3 multiply_convert_fusion
  158.9 0.0 copy-done.4
  159.0 0.0 copy-done.5
  159.0 0.0 copy-done.6
  159.0 1.8 fusion
  160.8 0.6 dynamic_slice.6
  161.4 0.0 all-to-all-done.1
  161.4 2.9 %fusion.23 = f32[128,1024]{1,0:T(8,128)} fusion(bf16[1024,128]{1,0:T(8,128)(2,1)S(1)} %bitcast.21, bf16[1024,1024]{1,0:T(8,128)(2,1)} %all-gather.5.cloned.1.call-done), kind=kOutput, calls=%fused_computation.43 | convolution fusion | flops 268435456 | bytes 2883584 | tf_op jit(solution)/shard_map/dot_general | solution.py:60
  164.2 19.0 %collective-permute-done = f32[256,512]{1,0:T(8,128)S(1)} collective-permute-done((f32[256,512]{1,0:T(8,128)}, f32[256,512]{1,0:T(8,128)S(1)}, u32[]{:S(2)}, u32[]{:S(2)}) %collective-permute-start) | collective-permute-done | bytes 524320 | tf_op jit(solution)/shard_map/ppermute | solution.py:85
  183.2 0.8 copy.33
  (9 shorter events, 0.1 us)
Async XLA Ops:
  7.2 53.3 %all-gather.3.cloned.1.call-start = ((), (), s32[]{:S(2)}) async-start(), calls=%async_computation.2 | async-start | bytes 2359296 | tf_op jit(solution)/shard_map/all_gather | solution.py:23
  13.7 46.8 %copy-start.2 = (bf16[128,1024]{1,0:T(8,128)(2,1)S(1)}, bf16[128,1024]{1,0:T(8,128)(2,1)}, u32[]{:S(2)}) copy-start(bf16[128,1024]{1,0:T(8,128)(2,1)} %param.7) | copy-start | bytes 786436
  13.7 81.4 %all-to-all-start = ((bf16[256,4,1024]{2,0,1:T(8,128)(2,1)}), bf16[256,4,1024]{2,0,1:T(8,128)(2,1)S(1)}, u32[]{:S(2)}, u32[]{:S(2)}) async-start(bf16[256,4,1024]{2,0,1:T(8,128)(2,1)} %copy.27), calls=%async_computation | async-start | bytes 4194304 | tf_op jit(solution)/shard_map/all_to_all | solution.py:22
  17.4 47.0 %copy-start.8 = (s32[128,7]{0,1:T(8,128)S(1)}, s32[128,7]{0,1:T(8,128)}, u32[]{:S(2)}) copy-start(s32[128,7]{0,1:T(8,128)} %param.11) | copy-start | bytes 10756
  17.4 47.0 %copy-start.9 = (s32[128,7]{0,1:T(8,128)S(1)}, s32[128,7]{0,1:T(8,128)}, u32[]{:S(2)}) copy-start(s32[128,7]{0,1:T(8,128)} %param.10) | copy-start | bytes 10756
  17.5 77.7 %copy-start.10 = (f32[128]{0:T(128)S(1)}, f32[128]{0:T(128)}, u32[]{:S(2)}) copy-start(f32[128]{0:T(128)} %param.13) | copy-start | bytes 1540
  17.5 77.7 %copy-start.3 = (bf16[128,1024]{1,0:T(8,128)(2,1)S(1)}, bf16[128,1024]{1,0:T(8,128)(2,1)}, u32[]{:S(2)}) copy-start(bf16[128,1024]{1,0:T(8,128)(2,1)} %param.7) | copy-start | bytes 786436
  17.5 85.1 %all-reduce.2.cloned.1.call-start = ((), (), s32[]{:S(2)}) async-start(), calls=%async_computation.3 | async-start | bytes 1048576 | tf_op jit(solution)/shard_map/psum | solution.py:37
  63.7 88.0 %all-gather.5.cloned.1.call-start = ((), (), s32[]{:S(2)}) async-start(), calls=%async_computation.4 | async-start | bytes 2359296 | tf_op jit(solution)/shard_map/all_gather | solution.py:24
  64.4 39.3 %copy-start.7 = (s32[128]{0:T(128)S(1)}, s32[128]{0:T(128)}, u32[]{:S(2)}) copy-start(s32[128]{0:T(128)} %param.12) | copy-start | bytes 1540
  107.2 54.2 %all-to-all-start.1 = ((bf16[128,8,128]{2,0,1:T(8,128)(2,1)}), bf16[128,8,128]{2,0,1:T(8,128)(2,1)S(1)}, u32[]{:S(2)}, u32[]{:S(2)}) async-start(bf16[128,8,128]{2,0,1:T(8,128)(2,1)} %copy_bitcast_fusion), calls=%async_computation.1 | async-start | bytes 524288 | tf_op jit(solution)/shard_map/all_to_all | solution.py:59
  151.7 1.9 %copy-start = (bf16[1024,1024]{1,0:T(8,128)(2,1)S(1)}, bf16[1024,1024]{1,0:T(8,128)(2,1)}, u32[]{:S(2)}) copy-start(bf16[1024,1024]{1,0:T(8,128)(2,1)} %all-gather.5.cloned.1.call-done) | copy-start | bytes 6291460
  153.6 5.0 %copy-start.1 = (f32[128,1024]{1,0:T(8,128)S(1)}, f32[128,1024]{1,0:T(8,128)}, u32[]{:S(2)}) copy-start(f32[128,1024]{1,0:T(8,128)} %all-reduce.2.cloned.1.call-done) | copy-start | bytes 1572868
  153.6 5.3 %copy-start.4 = (bf16[1024,1024]{1,0:T(8,128)(2,1)S(1)}, bf16[1024,1024]{1,0:T(8,128)(2,1)}, u32[]{:S(2)}) copy-start(bf16[1024,1024]{1,0:T(8,128)(2,1)} %all-gather.3.cloned.1.call-done) | copy-start | bytes 6291460
  153.6 5.3 %copy-start.5 = (bf16[128,1024]{1,0:T(8,128)(2,1)S(1)}, bf16[128,1024]{1,0:T(8,128)(2,1)}, u32[]{:S(2)}) copy-start(bf16[128,1024]{1,0:T(8,128)(2,1)} %get-tuple-element.6) | copy-start | bytes 786436
  153.6 5.4 %copy-start.6 = (bf16[128,1024]{1,0:T(8,128)(2,1)S(1)}, bf16[128,1024]{1,0:T(8,128)(2,1)}, u32[]{:S(2)}) copy-start(bf16[128,1024]{1,0:T(8,128)(2,1)} %get-tuple-element.7) | copy-start | bytes 786436
  154.9 28.3 %collective-permute-start = (f32[256,512]{1,0:T(8,128)}, f32[256,512]{1,0:T(8,128)S(1)}, u32[]{:S(2)}, u32[]{:S(2)}) collective-permute-start(f32[256,512]{1,0:T(8,128)} %convolution_add_fusion), channel_id=1, source_target_pairs={{0,0},{1,8},{2,16},{3,24},{4,4},{5,12},{6,20},{7,28},{8,1},{9,9},{... | collective-permute-start | bytes 1572872 | tf_op jit(solution)/shard_map/ppermute | solution.py:85
Sparse Core Ops, SparseCore 0:
  10.1 50.3 all-gather.2
  63.8 30.5 all-reduce.1
  96.6 55.0 all-gather.4
where the time goes:
time: 191 us
  blocking collectives  69.8 us (37%)
  waiting for transfers between devices  67.3 us (35%)
  between operations  14 us (7%)
  matrix products  11.8 us (6%)
  starting transfers between devices  11 us (6%)
  other arithmetic  9.43 us (5%)
  local copies, waits for them, and re-layouts  7.28 us (4%)
    all_gather x1, waiting for transfers between devices, per_device(): all_passages = lax.all_gather(passages, 'blk', axis=0, tiled=True)  42.9 us
    all_gather x1, blocking collectives, per_device(): all_hard = lax.all_gather(hard_grad, 'blk', axis=0, tiled=True)  33.2 us
    all_gather x1, blocking collectives, per_device(): all_ids = lax.all_gather(ids, 'blk', axis=0, tiled=True)  30.6 us
    ppermute x1, waiting for transfers between devices, per_device(): table_grad = lax.ppermute(piece, ('blk', 'corpus'), perm)  19 us
    psum x1, blocking collectives, per_device(): logits, hard_logits = lax.psum((logits, hard_logits), 'corpus')  5.93 us
    unnamed x24, local copies, waits for them, and re-layouts  4.18 us
    all_gather x1, waiting for transfers between devices, per_device(): all_queries = lax.all_gather(queries, 'blk', axis=0, tiled=True)  3.95 us
  transfers between devices with their start and end apart: 6, of which 3 were waited for; matrix products, arithmetic and copies ran while one was open for 14% of the time, Pallas kernels for 0%

commit v1 on v0

--- a/solution.py
+++ b/solution.py
@@ -20,7 +20,25 @@
     owner_index = lax.axis_index("corpus")
     blk_index = lax.axis_index("blk")
     table_cols = lax.all_to_all(table, "corpus", split_axis=1, concat_axis=0, tiled=True)
-    all_passages = lax.all_gather(passages, "blk", axis=0, tiled=True)
+    size, position, width = (lax.axis_size("blk"), lax.axis_index("blk"), passages.shape[0])
+    route = [(i, (i + 1) % size) for i in range(size)]
+    downward = [(i, (i - 1) % size) for i in range(size)]
+    all_passages = jnp.zeros(
+        (*passages.shape[:0], size * width, *passages.shape[0 + 1 :]), passages.dtype
+    )
+    all_passages = lax.dynamic_update_slice_in_dim(all_passages, passages, position * width, axis=0)
+    from_left = from_right = passages
+    middle = size // 2
+    for step in range(1, middle + 1):
+        from_left = lax.ppermute(from_left, "blk", route)
+        all_passages = lax.dynamic_update_slice_in_dim(
+            all_passages, from_left, (position - step) % size * width, axis=0
+        )
+        if step < size - middle:
+            from_right = lax.ppermute(from_right, "blk", downward)
+            all_passages = lax.dynamic_update_slice_in_dim(
+                all_passages, from_right, (position + step) % size * width, axis=0
+            )
     all_queries = lax.all_gather(queries, "blk", axis=0, tiled=True)
     ids = neg_owner * rows_shard + neg_row
     all_ids = lax.all_gather(ids, "blk", axis=0, tiled=True)

time: 191 us -> 185 us (0.969)
  waiting for transfers between devices: 67.3 us -> 45.8 us
  starting transfers between devices: 11 us -> 28.5 us
  blocking collectives: 69.8 us -> 65.2 us
  other arithmetic: 9.43 us -> 6.11 us
  local copies, waits for them, and re-layouts: 7.28 us -> 10.5 us
    all_gather x1 -> x0, waiting for transfers between devices: 42.9 us -> none  [per_device(): all_passages = lax.all_gather(passages, 'blk', axis=0, tiled=True)]
    ppermute x0 -> x7, waiting for transfers between devices: none -> 30.3 us  [the longest x4 30.3 us: per_device(): from_left = lax.ppermute(from_left, 'blk', route)]
    ppermute x0 -> x7, starting transfers between devices: none -> 18.2 us  [the longest x3 9.34 us: per_device(): from_right = lax.ppermute(from_right, 'blk', downward)]
    all_gather x1, blocking collectives: 33.2 us -> 28.3 us  [per_device(): all_hard = lax.all_gather(hard_grad, 'blk', axis=0, tiled=True)]
    ppermute x1, waiting for transfers between devices: 19 us -> 14.8 us  [per_device(): table_grad = lax.ppermute(piece, ('blk', 'corpus'), perm)]
    all_gather x1, waiting for transfers between devices: 3.95 us -> 0.03 us  [per_device(): all_queries = lax.all_gather(queries, 'blk', axis=0, tiled=True)]
    all_to_all x1 -> x0, other arithmetic: 2.05 us -> none  [per_device(): lax.all_to_all(soft_grad, 'blk', split_axis=1, concat_axis=0, tiled=True)]
    unnamed x24 -> x28, local copies, waits for them, and re-layouts: 4.18 us -> 4.97 us
  transfers between devices with their start and end apart: 6 -> 12, of which waited for: 3 -> 5; matrix products, arithmetic and copies ran while one was open for 14% -> 15% of each run, Pallas kernels for 0% -> 0%
where the time goes in v1:
time: 185 us
  blocking collectives  65.2 us (35%)
  waiting for transfers between devices  45.8 us (25%)
  starting transfers between devices  28.5 us (15%)
  between operations  15.9 us (9%)
  matrix products  12.7 us (7%)
  local copies, waits for them, and re-layouts  10.5 us (6%)
  other arithmetic  6.11 us (3%)
    all_gather x1, blocking collectives, per_device(): all_ids = lax.all_gather(ids, 'blk', axis=0, tiled=True)  30.8 us
    ppermute x4, waiting for transfers between devices, per_device(): from_left = lax.ppermute(from_left, 'blk', route)  30.3 us
    all_gather x1, blocking collectives, per_device(): all_hard = lax.all_gather(hard_grad, 'blk', axis=0, tiled=True)  28.3 us
    ppermute x1, waiting for transfers between devices, per_device(): table_grad = lax.ppermute(piece, ('blk', 'corpus'), perm)  14.8 us
    ppermute x3, starting transfers between devices, per_device(): from_right = lax.ppermute(from_right, 'blk', downward)  9.34 us
    ppermute x4, starting transfers between devices, per_device(): from_left = lax.ppermute(from_left, 'blk', route)  8.91 us
    psum x1, blocking collectives, per_device(): logits, hard_logits = lax.psum((logits, hard_logits), 'corpus')  6.08 us
    unnamed x28, local copies, waits for them, and re-layouts  4.97 us
  transfers between devices with their start and end apart: 12, of which 5 were waited for; matrix products, arithmetic and copies ran while one was open for 15% of the time, Pallas kernels for 0%

profile of v1, /device:TPU:2, one launch (start us, length us, event | category | flops | bytes accessed | tf_op | source)
XLA Modules:
  0.0 184.8 jit_solution(17547856445293310696)
XLA Ops:
  8.0 0.0 copy-start.6
  8.0 0.0 all-reduce.2.cloned.1.call-start
  8.1 1.6 collective-permute-start
  9.6 3.2 %collective-permute-start.1 = (bf16[128,1024]{1,0:T(8,128)(2,1)}, bf16[128,1024]{1,0:T(8,128)(2,1)S(1)}, u32[]{:S(2)}, u32[]{:S(2)}) collective-permute-start(bf16[128,1024]{1,0:T(8,128)(2,1)} %param.8), channel_id=1, source_target_pairs={{0,28},{4,0},{8,4},{12,8},{16,12},{20,16},{24,20},{28,24},{1,29},{... | collective-permute-start | bytes 786440 | tf_op jit(solution)/shard_map/ppermute | solution.py:38
  12.8 8.3 %collective-permute-done = bf16[128,1024]{1,0:T(8,128)(2,1)S(1)} collective-permute-done((bf16[128,1024]{1,0:T(8,128)(2,1)}, bf16[128,1024]{1,0:T(8,128)(2,1)S(1)}, u32[]{:S(2)}, u32[]{:S(2)}) %collective-permute-start) | collective-permute-done | bytes 262176 | tf_op jit(solution)/shard_map/ppermute | solution.py:33
  21.1 2.4 %collective-permute-start.2 = (bf16[128,1024]{1,0:T(8,128)(2,1)S(1)}, bf16[128,1024]{1,0:T(8,128)(2,1)S(1)}, u32[]{:S(2)}, u32[]{:S(2)}) collective-permute-start(bf16[128,1024]{1,0:T(8,128)(2,1)S(1)} %collective-permute-done), channel_id=1, source_target_pairs={{0,4},{4,8},{8,12},{12,16},{16,20},{20,24},{24,28},{28,0},{1,5},{5... | collective-permute-start | bytes 786440 | tf_op jit(solution)/shard_map/ppermute | solution.py:33
  23.5 0.0 collective-permute-done.1
  23.5 3.0 %collective-permute-start.3 = (bf16[128,1024]{1,0:T(8,128)(2,1)S(1)}, bf16[128,1024]{1,0:T(8,128)(2,1)}, u32[]{:S(2)}, u32[]{:S(2)}) collective-permute-start(bf16[128,1024]{1,0:T(8,128)(2,1)S(1)} %collective-permute-done.1), channel_id=1, source_target_pairs={{0,28},{4,0},{8,4},{12,8},{16,12},{20,16},{24,20},{28,24},{1,29},{... | collective-permute-start | bytes 786440 | tf_op jit(solution)/shard_map/ppermute | solution.py:38
  26.5 0.3 broadcast_in_dim.36
  26.8 0.0 copy-done.6
  26.8 0.0 copy-start.4
  27.0 6.8 %collective-permute-done.2 = bf16[128,1024]{1,0:T(8,128)(2,1)S(1)} collective-permute-done((bf16[128,1024]{1,0:T(8,128)(2,1)S(1)}, bf16[128,1024]{1,0:T(8,128)(2,1)S(1)}, u32[]{:S(2)}, u32[]{:S(2)}) %collective-permute-start.2) | collective-permute-done | bytes 262176 | tf_op jit(solution)/shard_map/ppermute | solution.py:33
  33.8 2.5 %collective-permute-start.4 = (bf16[128,1024]{1,0:T(8,128)(2,1)S(1)}, bf16[128,1024]{1,0:T(8,128)(2,1)S(1)}, u32[]{:S(2)}, u32[]{:S(2)}) collective-permute-start(bf16[128,1024]{1,0:T(8,128)(2,1)S(1)} %collective-permute-done.2), channel_id=1, source_target_pairs={{0,4},{4,8},{8,12},{12,16},{16,20},{20,24},{24,28},{28,0},{1,5},{5... | collective-permute-start | bytes 786440 | tf_op jit(solution)/shard_map/ppermute | solution.py:33
  36.4 0.0 collective-permute-done.3
  36.4 3.1 %collective-permute-start.5 = (bf16[128,1024]{1,0:T(8,128)(2,1)}, bf16[128,1024]{1,0:T(8,128)(2,1)S(1)}, u32[]{:S(2)}, u32[]{:S(2)}) collective-permute-start(bf16[128,1024]{1,0:T(8,128)(2,1)} %collective-permute-done.3), channel_id=1, source_target_pairs={{0,28},{4,0},{8,4},{12,8},{16,12},{20,16},{24,20},{28,24},{1,29},{... | collective-permute-start | bytes 786440 | tf_op jit(solution)/shard_map/ppermute | solution.py:38
  39.5 6.5 %collective-permute-done.4 = bf16[128,1024]{1,0:T(8,128)(2,1)S(1)} collective-permute-done((bf16[128,1024]{1,0:T(8,128)(2,1)S(1)}, bf16[128,1024]{1,0:T(8,128)(2,1)S(1)}, u32[]{:S(2)}, u32[]{:S(2)}) %collective-permute-start.4) | collective-permute-done | bytes 262176 | tf_op jit(solution)/shard_map/ppermute | solution.py:33
  46.0 2.5 %collective-permute-start.6 = (bf16[128,1024]{1,0:T(8,128)(2,1)S(1)}, bf16[128,1024]{1,0:T(8,128)(2,1)S(1)}, u32[]{:S(2)}, u32[]{:S(2)}) collective-permute-start(bf16[128,1024]{1,0:T(8,128)(2,1)S(1)} %collective-permute-done.4), channel_id=1, source_target_pairs={{0,4},{4,8},{8,12},{12,16},{16,20},{20,24},{24,28},{28,0},{1,5},{5... | collective-permute-start | bytes 786440 | tf_op jit(solution)/shard_map/ppermute | solution.py:33
  48.4 1.0 constant_dynamic-update-slice_fusion.3
  49.4 0.0 collective-permute-done.5
  49.5 8.7 %collective-permute-done.6 = bf16[128,1024]{1,0:T(8,128)(2,1)S(1)} collective-permute-done((bf16[128,1024]{1,0:T(8,128)(2,1)S(1)}, bf16[128,1024]{1,0:T(8,128)(2,1)S(1)}, u32[]{:S(2)}, u32[]{:S(2)}) %collective-permute-start.6) | collective-permute-done | bytes 262176 | tf_op jit(solution)/shard_map/ppermute | solution.py:33
  58.2 0.0 copy-done.4
  58.2 0.0 copy-start.2
  58.3 1.5 convolution_bitcast_fusion
  59.8 0.0 all-reduce.2.cloned.1.call-update
  59.8 4.1 %copy.21 = bf16[256,4096]{0,1:T(8,128)(2,1)} copy(bf16[256,4096]{1,0:T(8,128)(2,1)} %param.9) | data formatting | bytes 4194304 | tf_op args[2]
  63.9 0.0 copy-done.2
  63.9 0.0 copy-start.12
  63.9 4.3 %all-to-all-start = ((bf16[256,4,1024]{0,2,1:T(8,128)(2,1)}), bf16[256,4,1024]{0,2,1:T(8,128)(2,1)S(1)}, u32[]{:S(2)}, u32[]{:S(2)}) async-start(bf16[256,4,1024]{0,2,1:T(8,128)(2,1)} %bitcast.16), calls=%async_computation | async-start | bytes 4194304 | tf_op jit(solution)/shard_map/all_to_all | solution.py:22
  68.2 0.0 all-gather.2.cloned.1.call-start
  68.2 0.6 all-gather.2.cloned.1.call-update
  68.8 0.0 copy-done.9
  68.8 0.0 copy-done.10
  68.8 30.8 %all_gather.10 = s32[1024,7]{0,1:T(8,128)S(1)} all-gather(s32[128,7]{0,1:T(8,128)S(1)} %multiply_add_fusion), channel_id=1, replica_groups=mesh['blk'=8,'corpus'=4] {'blk'}, dimensions={0}, use_global_device_ids=true | all-gather | bytes 32256 | tf_op jit(solution)/shard_map/all_gather | solution.py:44
  99.6 0.0 copy-done.12
  99.6 0.0 all-reduce.2.cloned.1.call-done
  99.6 1.2 multiply_reduce_fusion
  100.8 0.0 all-to-all-done
  100.8 0.0 copy-start.5
  100.9 2.5 %copy.22 = bf16[4,256,1024]{2,1,0:T(8,128)(2,1)} copy(bf16[4,256,1024]{1,2,0:T(8,128)(2,1)S(1)} %bitcast.15) | data formatting | bytes 4194304 | tf_op jit(solution)/shard_map/all_to_all | solution.py:22
  103.4 0.0 copy-done.5
  103.4 2.5 %fusion.21 = f32[128,1024]{1,0:T(8,128)S(1)} fusion(bf16[128,1024]{1,0:T(8,128)(2,1)S(1)} %copy-done.5, bf16[1024,1024]{1,0:T(8,128)(2,1)} %bitcast.17), kind=kOutput, calls=%fused_computation.49 | convolution fusion | flops 268435456 | bytes 2883584 | tf_op jit(solution)/shard_map/dot_general | solution.py:49
  105.9 0.6 select_reduce_fusion.2
  106.5 6.1 %psum.15 = f32[128,7]{0,1:T(8,128)S(1)} all-reduce(f32[128,7]{0,1:T(8,128)S(1)} %select_reduce_fusion.2), channel_id=1, replica_groups=mesh['blk'=8,'corpus'=4] {'corpus'}, use_global_device_ids=true, to_apply=%region_3.4 | all-reduce | flops 896 | bytes 7168 | tf_op jit(solution)/shard_map/psum | solution.py:55
  112.6 0.2 select_reduce_fusion.3
  112.8 0.5 select_reduce_fusion.1
  113.3 0.2 copy.23
  113.5 0.2 multiply_convert_fusion
  113.7 0.9 copy.25
  114.6 4.0 %all-to-all-start.1 = ((bf16[128,8,128]{2,0,1:T(8,128)(2,1)}), bf16[128,8,128]{2,0,1:T(8,128)(2,1)}, u32[]{:S(2)}, u32[]{:S(2)}) async-start(bf16[128,8,128]{2,0,1:T(8,128)(2,1)} %copy.25), calls=%async_computation.1 | async-start | bytes 524288 | tf_op jit(solution)/shard_map/all_to_all | solution.py:77
  118.6 28.3 %all_gather.11 = bf16[1024,7]{0,1:T(8,128)(2,1)S(1)} all-gather(bf16[128,7]{0,1:T(8,128)(2,1)S(1)} %get-tuple-element.9), channel_id=1, replica_groups=mesh['blk'=8,'corpus'=4] {'blk'}, dimensions={0}, use_global_device_ids=true | all-gather | bytes 16128 | tf_op jit(solution)/shard_map/all_gather | solution.py:81
  146.9 0.9 subtract_convert_fusion.2
  147.8 2.5 %select_reduce_fusion = f32[1024,256]{1,0:T(8,128)S(1)} fusion(f32[1024,7]{0,1:T(8,128)S(1)} %convert_element_type.40, s32[256]{0:T(256)S(1)} %iota_add_fusion, s32[1024,7]{0,1:T(8,128)S(1)} %all_gather.10), kind=kLoop, calls=%fused_computation | loop fusion | flops 5242880 | bytes 1106944 | tf_op jit(solution)/shard_map/reduce_sum | solution.py:88
  150.3 0.0 all-gather.2.cloned.1.call-done
  150.4 0.0 copy-start
  150.4 1.8 fusion.7
  152.2 0.0 copy-done
  152.3 1.3 convolution_add_fusion
  153.6 1.9 %collective-permute-start.7 = (f32[256,512]{1,0:T(8,128)}, f32[256,512]{1,0:T(8,128)S(1)}, u32[]{:S(2)}, u32[]{:S(2)}) collective-permute-start(f32[256,512]{1,0:T(8,128)} %convolution_add_fusion), channel_id=1, source_target_pairs={{0,0},{1,8},{2,16},{3,24},{4,4},{5,12},{6,20},{7,28},{8,1},{9,9},{... | collective-permute-start | bytes 1572872 | tf_op jit(solution)/shard_map/ppermute | solution.py:103
  155.5 3.4 %fusion = f32[128,1024]{1,0:T(8,128)} fusion(bf16[1024,1024]{1,0:T(8,128)(2,1)S(1)} %bitcast.18, bf16[1024,1024]{1,0:T(8,128)(2,1)} %copy-done.2, bf16[128,1024]{0,1:T(8,128)(2,1)S(1)} %copy-done.7, bf16[128,1024]{0,1:T(8,128)(2,1)S(1)} %copy-done.8, bf16[128,1024]{0,1:T(8,128)(2,1)S(1)} %multiply_convert_fusion), kind=kOutput, calls=%fused_computation.1 | convolution fusion | flops 826540032 | bytes 5505024 | tf_op jit(solution)/shard_map/dot_general | solution.py:76
  158.9 0.6 dynamic_slice.6
  159.5 0.0 all-to-all-done.1
  159.5 2.2 %fusion.22 = f32[128,1024]{1,0:T(8,128)} fusion(bf16[1024,128]{1,0:T(8,128)(2,1)} %bitcast.6, bf16[1024,1024]{1,0:T(8,128)(2,1)S(1)} %copy-done), kind=kOutput, calls=%fused_computation.50 | convolution fusion | flops 268435456 | bytes 2883584 | tf_op jit(solution)/shard_map/dot_general | solution.py:78
  161.7 14.8 %collective-permute-done.7 = f32[256,512]{1,0:T(8,128)S(1)} collective-permute-done((f32[256,512]{1,0:T(8,128)}, f32[256,512]{1,0:T(8,128)S(1)}, u32[]{:S(2)}, u32[]{:S(2)}) %collective-permute-start.7) | collective-permute-done | bytes 524320 | tf_op jit(solution)/shard_map/ppermute | solution.py:103
  176.5 0.8 copy.36
  (28 shorter events, 0.3 us)
Async XLA Ops:
  8.0 18.8 %copy-start.6 = (bf16[128,1024]{1,0:T(8,128)(2,1)S(1)}, bf16[128,1024]{1,0:T(8,128)(2,1)}, u32[]{:S(2)}) copy-start(bf16[128,1024]{1,0:T(8,128)(2,1)} %param.8) | copy-start | bytes 786436
  8.0 91.6 %all-reduce.2.cloned.1.call-start = ((), (), s32[]{:S(2)}) async-start(), calls=%async_computation.2 | async-start | bytes 1048576 | tf_op jit(solution)/shard_map/psum | solution.py:55
  8.1 13.1 %collective-permute-start = (bf16[128,1024]{1,0:T(8,128)(2,1)}, bf16[128,1024]{1,0:T(8,128)(2,1)S(1)}, u32[]{:S(2)}, u32[]{:S(2)}) collective-permute-start(bf16[128,1024]{1,0:T(8,128)(2,1)} %param.8), channel_id=1, source_target_pairs={{0,4},{4,8},{8,12},{12,16},{16,20},{20,24},{24,28},{28,0},{1,5},{5... | collective-permute-start | bytes 786440 | tf_op jit(solution)/shard_map/ppermute | solution.py:33
  9.6 13.9 %collective-permute-start.1 = (bf16[128,1024]{1,0:T(8,128)(2,1)}, bf16[128,1024]{1,0:T(8,128)(2,1)S(1)}, u32[]{:S(2)}, u32[]{:S(2)}) collective-permute-start(bf16[128,1024]{1,0:T(8,128)(2,1)} %param.8), channel_id=1, source_target_pairs={{0,28},{4,0},{8,4},{12,8},{16,12},{20,16},{24,20},{28,24},{1,29},{... | collective-permute-start | bytes 786440 | tf_op jit(solution)/shard_map/ppermute | solution.py:38
  21.1 12.7 %collective-permute-start.2 = (bf16[128,1024]{1,0:T(8,128)(2,1)S(1)}, bf16[128,1024]{1,0:T(8,128)(2,1)S(1)}, u32[]{:S(2)}, u32[]{:S(2)}) collective-permute-start(bf16[128,1024]{1,0:T(8,128)(2,1)S(1)} %collective-permute-done), channel_id=1, source_target_pairs={{0,4},{4,8},{8,12},{12,16},{16,20},{20,24},{24,28},{28,0},{1,5},{5... | collective-permute-start | bytes 786440 | tf_op jit(solution)/shard_map/ppermute | solution.py:33
  23.5 12.9 %collective-permute-start.3 = (bf16[128,1024]{1,0:T(8,128)(2,1)S(1)}, bf16[128,1024]{1,0:T(8,128)(2,1)}, u32[]{:S(2)}, u32[]{:S(2)}) collective-permute-start(bf16[128,1024]{1,0:T(8,128)(2,1)S(1)} %collective-permute-done.1), channel_id=1, source_target_pairs={{0,28},{4,0},{8,4},{12,8},{16,12},{20,16},{24,20},{28,24},{1,29},{... | collective-permute-start | bytes 786440 | tf_op jit(solution)/shard_map/ppermute | solution.py:38
  26.8 31.4 %copy-start.4 = (bf16[128,1024]{1,0:T(8,128)(2,1)S(1)}, bf16[128,1024]{1,0:T(8,128)(2,1)}, u32[]{:S(2)}) copy-start(bf16[128,1024]{1,0:T(8,128)(2,1)} %param.7) | copy-start | bytes 786436
  33.8 12.1 %collective-permute-start.4 = (bf16[128,1024]{1,0:T(8,128)(2,1)S(1)}, bf16[128,1024]{1,0:T(8,128)(2,1)S(1)}, u32[]{:S(2)}, u32[]{:S(2)}) collective-permute-start(bf16[128,1024]{1,0:T(8,128)(2,1)S(1)} %collective-permute-done.2), channel_id=1, source_target_pairs={{0,4},{4,8},{8,12},{12,16},{16,20},{20,24},{24,28},{28,0},{1,5},{5... | collective-permute-start | bytes 786440 | tf_op jit(solution)/shard_map/ppermute | solution.py:33
  36.4 13.1 %collective-permute-start.5 = (bf16[128,1024]{1,0:T(8,128)(2,1)}, bf16[128,1024]{1,0:T(8,128)(2,1)S(1)}, u32[]{:S(2)}, u32[]{:S(2)}) collective-permute-start(bf16[128,1024]{1,0:T(8,128)(2,1)} %collective-permute-done.3), channel_id=1, source_target_pairs={{0,28},{4,0},{8,4},{12,8},{16,12},{20,16},{24,20},{28,24},{1,29},{... | collective-permute-start | bytes 786440 | tf_op jit(solution)/shard_map/ppermute | solution.py:38
  46.0 12.2 %collective-permute-start.6 = (bf16[128,1024]{1,0:T(8,128)(2,1)S(1)}, bf16[128,1024]{1,0:T(8,128)(2,1)S(1)}, u32[]{:S(2)}, u32[]{:S(2)}) collective-permute-start(bf16[128,1024]{1,0:T(8,128)(2,1)S(1)} %collective-permute-done.4), channel_id=1, source_target_pairs={{0,4},{4,8},{8,12},{12,16},{16,20},{20,24},{24,28},{28,0},{1,5},{5... | collective-permute-start | bytes 786440 | tf_op jit(solution)/shard_map/ppermute | solution.py:33
  58.2 5.6 %copy-start.2 = (bf16[1024,1024]{1,0:T(8,128)(2,1)}, bf16[1024,1024]{1,0:T(8,128)(2,1)S(1)}, u32[]{:S(2)}) copy-start(bf16[1024,1024]{1,0:T(8,128)(2,1)S(1)} %constant_dynamic-update-slice_fusion) | copy-start | bytes 6291460
  63.9 4.9 %copy-start.9 = (s32[128,7]{0,1:T(8,128)S(1)}, s32[128,7]{0,1:T(8,128)}, u32[]{:S(2)}) copy-start(s32[128,7]{0,1:T(8,128)} %param.11) | copy-start | bytes 10756
  63.9 4.9 %copy-start.10 = (s32[128,7]{0,1:T(8,128)S(1)}, s32[128,7]{0,1:T(8,128)}, u32[]{:S(2)}) copy-start(s32[128,7]{0,1:T(8,128)} %param.10) | copy-start | bytes 10756
  63.9 35.7 %copy-start.12 = (f32[128]{0:T(128)S(1)}, f32[128]{0:T(128)}, u32[]{:S(2)}) copy-start(f32[128]{0:T(128)} %param.13) | copy-start | bytes 1540
  63.9 36.9 %all-to-all-start = ((bf16[256,4,1024]{0,2,1:T(8,128)(2,1)}), bf16[256,4,1024]{0,2,1:T(8,128)(2,1)S(1)}, u32[]{:S(2)}, u32[]{:S(2)}) async-start(bf16[256,4,1024]{0,2,1:T(8,128)(2,1)} %bitcast.16), calls=%async_computation | async-start | bytes 4194304 | tf_op jit(solution)/shard_map/all_to_all | solution.py:22
  68.2 82.2 %all-gather.2.cloned.1.call-start = ((), (), s32[]{:S(2)}) async-start(), calls=%async_computation.3 | async-start | bytes 2359296 | tf_op jit(solution)/shard_map/all_gather | solution.py:42
  100.8 2.6 %copy-start.5 = (bf16[128,1024]{1,0:T(8,128)(2,1)S(1)}, bf16[128,1024]{1,0:T(8,128)(2,1)}, u32[]{:S(2)}) copy-start(bf16[128,1024]{1,0:T(8,128)(2,1)} %param.7) | copy-start | bytes 786436
  103.4 9.2 %copy-start.3 = (f32[128,1024]{0,1:T(8,128)S(1)}, f32[128,1024]{0,1:T(8,128)}, u32[]{:S(2)}) copy-start(f32[128,1024]{0,1:T(8,128)} %all-reduce.2.cloned.1.call-done) | copy-start | bytes 1572868
  103.4 9.2 %copy-start.11 = (s32[128]{0:T(128)S(1)}, s32[128]{0:T(128)}, u32[]{:S(2)}) copy-start(s32[128]{0:T(128)} %param.12) | copy-start | bytes 1540
  114.6 44.9 %all-to-all-start.1 = ((bf16[128,8,128]{2,0,1:T(8,128)(2,1)}), bf16[128,8,128]{2,0,1:T(8,128)(2,1)}, u32[]{:S(2)}, u32[]{:S(2)}) async-start(bf16[128,8,128]{2,0,1:T(8,128)(2,1)} %copy.25), calls=%async_computation.1 | async-start | bytes 524288 | tf_op jit(solution)/shard_map/all_to_all | solution.py:77
  150.4 1.9 %copy-start = (bf16[1024,1024]{1,0:T(8,128)(2,1)S(1)}, bf16[1024,1024]{1,0:T(8,128)(2,1)}, u32[]{:S(2)}) copy-start(bf16[1024,1024]{1,0:T(8,128)(2,1)} %all-gather.2.cloned.1.call-done) | copy-start | bytes 6291460
  152.3 3.2 %copy-start.1 = (bf16[4,256,1024]{2,1,0:T(8,128)(2,1)S(1)}, bf16[4,256,1024]{2,1,0:T(8,128)(2,1)}, u32[]{:S(2)}) copy-start(bf16[4,256,1024]{2,1,0:T(8,128)(2,1)} %copy.22) | copy-start | bytes 6291460
  152.3 3.2 %copy-start.7 = (bf16[128,1024]{0,1:T(8,128)(2,1)S(1)}, bf16[128,1024]{0,1:T(8,128)(2,1)}, u32[]{:S(2)}) copy-start(bf16[128,1024]{0,1:T(8,128)(2,1)} %get-tuple-element.6) | copy-start | bytes 786436
  152.3 3.2 %copy-start.8 = (bf16[128,1024]{0,1:T(8,128)(2,1)S(1)}, bf16[128,1024]{0,1:T(8,128)(2,1)}, u32[]{:S(2)}) copy-start(bf16[128,1024]{0,1:T(8,128)(2,1)} %get-tuple-element.7) | copy-start | bytes 786436
  153.6 23.0 %collective-permute-start.7 = (f32[256,512]{1,0:T(8,128)}, f32[256,512]{1,0:T(8,128)S(1)}, u32[]{:S(2)}, u32[]{:S(2)}) collective-permute-start(f32[256,512]{1,0:T(8,128)} %convolution_add_fusion), channel_id=1, source_target_pairs={{0,0},{1,8},{2,16},{3,24},{4,4},{5,12},{6,20},{7,28},{8,1},{9,9},{... | collective-permute-start | bytes 1572872 | tf_op jit(solution)/shard_map/ppermute | solution.py:103
Sparse Core Ops, SparseCore 0:
  59.9 34.1 all-reduce.1
Sparse Core Ops, SparseCore 1:
  70.8 47.7 all-gather.1
